TPU v7x, 512 devices: a whole 4x8x8 slice. The times are simulated.
512 devices in a mesh: dp: 16 (over z, core), mp: 32 (over x, y).
Axes of the slice: x: 4, y: 8, z: 8, core: 2. Of those that a mesh axis runs over, the one named last changes fastest.
Arguments:
- tokens: bfloat16 [2048, 4096], P(('dp', 'mp')), may hold values from -6 to 6
- hidden_grad: bfloat16 [2048, 14336], P('dp', 'mp'), may hold values from -0.125 to 0.125
- gate_weight: bfloat16 [4096, 14336], P('dp', 'mp'), may hold values from -0.09375 to 0.09375
- up_weight: bfloat16 [4096, 14336], P('dp', 'mp'), may hold values from -0.09375 to 0.09375
- gate_probe: bfloat16 [4096, 14336], P('dp', 'mp'), may hold values from -1 to 1, as said below
- gate_mean: float32 [4096, 14336], P('dp', 'mp'), may hold values from -0.6 to 0.6
- gate_curve: float32 [4096, 14336], P('dp', 'mp'), may hold values from 1 to 10
- group_counts: int32 [16], replicated, may hold values from 32 to 128, as said below
Outputs:
- gate_weight_new: bfloat16 [4096, 14336], P('dp', 'mp')
- gate_mean_new: float32 [4096, 14336], P('dp', 'mp')
- gate_curve_new: float32 [4096, 14336], P('dp', 'mp')
Inputs may be any that keep to these rules, and one draw needn't show every extreme that they name: `group_counts`: some data group has exactly 128 live tokens in every draw. `gate_probe`: every entry is -1 or 1, each sign drawn independently.
All inputs are finite; a program needn't handle non-finite values.
Results may differ from a plain program's by a relative error of at most 0.0017.
Values may be sent and summed in bfloat16 or wider, within the bound.
No kernel may reach another device: no remote copies, remote signals or barrier semaphores. Data moves between devices by JAX's collectives and lax.ppermute only.
A program may use at most 64 MiB of HBM per device.

v0:
```python
import jax
import jax.numpy as jnp
from jax import lax
from jax.sharding import PartitionSpec as P

first_decay = 0.9
second_decay = 0.999
learn_rate = 0.15
epsilon_term = 0.0001
first_fix = 1.0 - 0.9**10
second_fix = 1.0 - 0.999**10


def silu_parts(inputs):
    sigmoid_part = jax.nn.sigmoid(inputs)
    silu_slope = sigmoid_part * (1.0 + inputs * (1.0 - sigmoid_part))
    silu_bend = sigmoid_part * (1.0 - sigmoid_part) * (2.0 + inputs * (1.0 - 2.0 * sigmoid_part))
    return (silu_slope, silu_bend)


def adahessian(weight, mean_old, curve_old, gradient, probe_value, product):
    diagonal = probe_value.astype(jnp.float32) * product
    mean_new = first_decay * mean_old + (1.0 - first_decay) * gradient
    curve_new = second_decay * curve_old + (1.0 - second_decay) * diagonal * diagonal
    step_ratio = mean_new / first_fix / (jnp.sqrt(curve_new / second_fix) + epsilon_term)
    weight_new = (weight.astype(jnp.float32) - learn_rate * step_ratio).astype(jnp.bfloat16)
    return (weight_new, mean_new, curve_new)


DP = ("z", "c")
MP = ("x", "y")


def chip_ring(x, n_dp):
    n_chip = n_dp // 2
    d = lax.axis_index(DP)
    z = d // 2
    c = d % 2
    rows = x.shape[0]
    partner = [(i, i ^ 1) for i in range(n_dp)]
    ring = [(2 * j, 2 * ((j + 1) % n_chip)) for j in range(n_chip)] + [
        (2 * j + 1, 2 * ((j - 1) % n_chip) + 1) for j in range(n_chip)
    ]
    px = lax.ppermute(x, DP, partner)
    pieces = [(x, d), (px, d ^ 1)]
    cur = jnp.concatenate([x, px], 0)
    step = 2 * c - 1
    for k in range(1, n_chip // 2 + 1):
        cur = lax.ppermute(cur, DP, ring)
        j = (z + k * step) % n_chip
        o = c
        pieces.append((cur[:rows], 2 * j + o))
        pieces.append((cur[rows:], 2 * j + 1 - o))
        if k < n_chip // 2:
            ex = lax.ppermute(cur, DP, partner)
            j2 = (z - k * step) % n_chip
            o2 = 1 - c
            pieces.append((ex[:rows], 2 * j2 + o2))
            pieces.append((ex[rows:], 2 * j2 + 1 - o2))
    return pieces


def body(
    tokens, hidden_grad, gate_weight, up_weight, gate_probe, gate_mean, gate_curve, group_counts
):
    n_dp = lax.axis_size(DP)
    n_mp = lax.axis_size(MP)
    rows_loc, feat = tokens.shape
    shard = feat // n_dp
    width = gate_weight.shape[1]
    d = lax.axis_index(DP)

    def gather_mp(a):
        a = lax.all_gather(a, "y", axis=0, tiled=True)
        return lax.all_gather(a, "x", axis=0, tiled=True)

    whole = gather_mp(tokens)
    group_rows = whole.shape[0]
    t3 = tokens.reshape(rows_loc, n_dp, shard)
    a2a = lax.all_to_all(t3, DP, split_axis=1, concat_axis=1, tiled=True)
    cols = (
        gather_mp(a2a)
        .reshape(n_mp, rows_loc, n_dp, shard)
        .transpose(2, 0, 1, 3)
        .reshape(n_dp * group_rows, shard)
    )
    w3 = jnp.concatenate([gate_weight, up_weight, gate_probe], 1)
    pre = None
    for piece, s in chip_ring(w3, n_dp):
        part = lax.dynamic_slice_in_dim(whole, s * shard, shard, axis=1)
        term = jnp.dot(part, piece, preferred_element_type=jnp.float32)
        pre = term if pre is None else pre + term
    gate_pre = pre[:, :width]
    up_pre = pre[:, width : 2 * width]
    gate_tan = pre[:, 2 * width :]
    limit = lax.dynamic_index_in_dim(group_counts, d, 0, keepdims=False)
    live = (jnp.arange(group_rows, dtype=jnp.int32) < limit).astype(jnp.float32)
    silu_slope, silu_bend = silu_parts(gate_pre)
    masked = hidden_grad.astype(jnp.float32) * live[:, None]
    grad_gate = (masked * up_pre * silu_slope).astype(jnp.bfloat16)
    tan_gate = (masked * up_pre * silu_bend * gate_tan).astype(jnp.bfloat16)
    packed = jnp.concatenate([grad_gate, tan_gate], 1)
    sums = None
    for piece, g in chip_ring(packed, n_dp):
        part = lax.dynamic_slice_in_dim(cols, g * group_rows, group_rows, axis=0)
        term = lax.dot_general(
            part, piece, (((0,), (0,)), ((), ())), preferred_element_type=jnp.float32
        )
        sums = term if sums is None else sums + term
    gate_out = adahessian(
        gate_weight, gate_mean, gate_curve, sums[:, :width], gate_probe, sums[:, width:]
    )
    return (gate_out[0], gate_out[1], gate_out[2])


def solution(mesh):
    n_dp, n_mp = mesh.devices.shape
    n_x = len({dev.coords[0] for dev in mesh.devices[0]})
    mesh4 = jax.sharding.Mesh(
        mesh.devices.reshape(n_dp // 2, 2, n_x, n_mp // n_x), ("z", "c", "x", "y")
    )
    every = DP + MP
    return jax.shard_map(
        body,
        mesh=mesh4,
        in_specs=(
            P(every, None),
            P(DP, MP),
            P(DP, MP),
            P(DP, MP),
            P(DP, MP),
            P(DP, MP),
            P(DP, MP),
            P(),
        ),
        out_specs=(P(DP, MP), P(DP, MP), P(DP, MP)),
        check_vma=False,
    )
```

profile of v0, /device:TPU:4, one launch (start us, length us, event | category | flops | bytes accessed | tf_op | source)
XLA Modules:
  0.0 219.7 jit_solution(13233006125582500672)
XLA Ops:
  7.2 1.0 constant_dynamic-update-slice_fusion.2
  8.2 1.0 constant_dynamic-update-slice_fusion.1
  9.1 1.0 constant_dynamic-update-slice_fusion
  10.1 1.9 collective-permute-start
  12.0 2.1 collective-permute-done
  14.2 4.3 %collective-permute-start.1 = (bf16[512,1344]{0,1:T(8,128)(2,1)S(1)}, bf16[512,1344]{0,1:T(8,128)(2,1)}, u32[]{:S(2)}, u32[]{:S(2)}) collective-permute-start(bf16[512,1344]{0,1:T(8,128)(2,1)S(1)} %pad_maximum_fusion), channel_id=1, source_target_pairs={{0,64},{64,128},{128,192},{192,256},{256,320},{320,384},{384,448},... | collective-permute-start | bytes 4128776 | tf_op jit(solution)/shard_map/ppermute | solution.py:49
  18.5 26.6 %all-gather = bf16[8,4,4096]{2,1,0:T(4,128)(2,1)S(1)} all-gather(bf16[1,4,4096]{2,1,0:T(4,128)(2,1)} %bitcast.4), channel_id=1, replica_groups=mesh['z'=8,'c'=2,'x'=4,'y'=8] {'y'}, dimensions={0}, use_global_device_ids=true | all-gather | bytes 294912 | tf_op jit(solution)/shard_map/all_gather | solution.py:74
  45.1 0.8 reshape.24
  45.9 4.4 %collective-permute-start.3 = (bf16[512,1344]{0,1:T(8,128)(2,1)}, bf16[512,1344]{0,1:T(8,128)(2,1)S(1)}, u32[]{:S(2)}, u32[]{:S(2)}) collective-permute-start(bf16[512,1344]{0,1:T(8,128)(2,1)} %collective-permute-done.1), channel_id=1, source_target_pairs={{0,64},{64,128},{128,192},{192,256},{256,320},{320,384},{384,448},... | collective-permute-start | bytes 4128776 | tf_op jit(solution)/shard_map/ppermute | solution.py:49
  50.3 8.6 %all-to-all-start = ((bf16[4,16,256]{2,0,1:T(4,128)(2,1)}), bf16[4,16,256]{2,0,1:T(4,128)(2,1)S(1)}, u32[]{:S(2)}, u32[]{:S(2)}) async-start(bf16[4,16,256]{2,0,1:T(4,128)(2,1)} %bitcast), calls=%async_computation | async-start | bytes 65536 | tf_op jit(solution)/shard_map/all_to_all | solution.py:80
  59.8 0.6 compare_convert_fusion
  60.4 14.0 %all-to-all-done = bf16[4,16,256]{2,0,1:T(4,128)(2,1)S(1)} async-done(((bf16[4,16,256]{2,0,1:T(4,128)(2,1)}), bf16[4,16,256]{2,0,1:T(4,128)(2,1)S(1)}, u32[]{:S(2)}, u32[]{:S(2)}) %all-to-all-start) | async-done | bytes 32800 | tf_op jit(solution)/shard_map/all_to_all | solution.py:80
  74.5 26.8 %all_gather.12 = bf16[32,16,256]{2,1,0:T(8,128)(2,1)} all-gather(bf16[4,16,256]{2,1,0:T(8,128)(2,1)S(1)} %copy.28), channel_id=1, replica_groups=mesh['z'=8,'c'=2,'x'=4,'y'=8] {'y'}, dimensions={0}, use_global_device_ids=true | all-gather | bytes 294912 | tf_op jit(solution)/shard_map/all_gather | solution.py:74
  101.3 1.9 collective-permute-start.2
  103.2 1.3 fusion.108
  104.5 1.9 collective-permute-start.5
  106.8 1.4 fusion.41
  108.3 1.5 fusion
  109.7 2.6 %collective-permute-start.4 = (bf16[512,1344]{0,1:T(8,128)(2,1)S(1)}, bf16[512,1344]{0,1:T(8,128)(2,1)S(1)}, u32[]{:S(2)}, u32[]{:S(2)}) collective-permute-start(bf16[512,1344]{0,1:T(8,128)(2,1)S(1)} %collective-permute-done.3), channel_id=1, source_target_pairs={{0,32},{32,0},{64,96},{96,64},{128,160},{160,128},{192,224},{224,1... | collective-permute-start | bytes 4128776 | tf_op jit(solution)/shard_map/ppermute | solution.py:55
  113.1 1.4 fusion.38
  114.5 11.4 %collective-permute-done.5 = bf16[512,1344]{0,1:T(8,128)(2,1)S(1)} collective-permute-done((bf16[512,1344]{0,1:T(8,128)(2,1)S(1)}, bf16[512,1344]{0,1:T(8,128)(2,1)S(1)}, u32[]{:S(2)}, u32[]{:S(2)}) %collective-permute-start.5) | collective-permute-done | bytes 1376288 | tf_op jit(solution)/shard_map/ppermute | solution.py:49
  125.9 1.9 collective-permute-start.7
  127.9 1.5 fusion.3
  129.3 1.9 collective-permute-start.6
  132.7 14.7 %collective-permute-done.7 = bf16[512,1344]{0,1:T(8,128)(2,1)S(1)} collective-permute-done((bf16[512,1344]{0,1:T(8,128)(2,1)S(1)}, bf16[512,1344]{0,1:T(8,128)(2,1)S(1)}, u32[]{:S(2)}, u32[]{:S(2)}) %collective-permute-start.7) | collective-permute-done | bytes 1376288 | tf_op jit(solution)/shard_map/ppermute | solution.py:49
  149.5 2.1 collective-permute-start.8
  151.6 1.6 collective-permute-done.8
  153.2 1.8 pad_maximum_fusion.1
  154.9 1.9 collective-permute-start.9
  157.0 0.8 copy.26
  157.8 0.8 copy.31
  159.2 1.8 copy.36
  161.6 1.3 convolution_add_fusion.9
  162.9 4.0 %collective-permute-done.9 = bf16[256,896]{0,1:T(8,128)(2,1)} collective-permute-done((bf16[256,896]{0,1:T(8,128)(2,1)}, bf16[256,896]{0,1:T(8,128)(2,1)}, u32[]{:S(2)}, u32[]{:S(2)}) %collective-permute-start.9) | collective-permute-done | bytes 458784 | tf_op jit(solution)/shard_map/ppermute | solution.py:49
  166.8 1.9 collective-permute-start.10
  168.7 1.9 collective-permute-start.11
  170.7 1.3 fusion.75
  171.9 1.3 fusion.19
  173.2 7.3 %collective-permute-done.11 = bf16[256,896]{0,1:T(8,128)(2,1)S(1)} collective-permute-done((bf16[256,896]{0,1:T(8,128)(2,1)}, bf16[256,896]{0,1:T(8,128)(2,1)S(1)}, u32[]{:S(2)}, u32[]{:S(2)}) %collective-permute-start.11) | collective-permute-done | bytes 458784 | tf_op jit(solution)/shard_map/ppermute | solution.py:49
  180.5 1.9 collective-permute-start.12
  182.5 1.9 collective-permute-start.13
  185.7 8.3 %collective-permute-done.13 = bf16[256,896]{0,1:T(8,128)(2,1)S(1)} collective-permute-done((bf16[256,896]{0,1:T(8,128)(2,1)S(1)}, bf16[256,896]{0,1:T(8,128)(2,1)S(1)}, u32[]{:S(2)}, u32[]{:S(2)}) %collective-permute-start.13) | collective-permute-done | bytes 458784 | tf_op jit(solution)/shard_map/ppermute | solution.py:49
  194.0 1.9 collective-permute-start.14
  196.0 2.1 collective-permute-start.15
  199.5 8.1 %collective-permute-done.15 = bf16[256,896]{0,1:T(8,128)(2,1)S(1)} collective-permute-done((bf16[256,896]{0,1:T(8,128)(2,1)S(1)}, bf16[256,896]{0,1:T(8,128)(2,1)S(1)}, u32[]{:S(2)}, u32[]{:S(2)}) %collective-permute-start.15) | collective-permute-done | bytes 458784 | tf_op jit(solution)/shard_map/ppermute | solution.py:49
  210.1 1.0 copy.33
  211.1 1.0 copy.34
  212.0 0.8 copy.32
  (65 shorter events, 11.7 us)
Async XLA Ops:
  7.2 96.1 %all-gather.6.cloned.1.call-start = ((), (), s32[]{:S(2)}) async-start(), calls=%async_computation.2 | async-start | bytes 1310720 | tf_op jit(solution)/shard_map/all_gather | solution.py:75
  10.1 4.0 %collective-permute-start = (bf16[256,1344]{0,1:T(8,128)(2,1)S(1)}, bf16[256,1344]{0,1:T(8,128)(2,1)S(1)}, u32[]{:S(2)}, u32[]{:S(2)}) collective-permute-start(bf16[256,1344]{0,1:T(8,128)(2,1)S(1)} %constant_dynamic-update-slice_fusion), channel_id=1, source_target_pairs={{0,32},{32,0},{64,96},{96,64},{128,160},{160,128},{192,224},{224,1... | collective-permute-start | bytes 2064392 | tf_op jit(solution)/shard_map/ppermute | solution.py:44
  14.2 45.0 %copy-start.8 = (s32[16]{0:T(128)S(1)}, s32[16]{0:T(128)}, u32[]{:S(2)}) copy-start(s32[16]{0:T(128)} %param.15) | copy-start | bytes 196
  14.2 31.7 %collective-permute-start.1 = (bf16[512,1344]{0,1:T(8,128)(2,1)S(1)}, bf16[512,1344]{0,1:T(8,128)(2,1)}, u32[]{:S(2)}, u32[]{:S(2)}) collective-permute-start(bf16[512,1344]{0,1:T(8,128)(2,1)S(1)} %pad_maximum_fusion), channel_id=1, source_target_pairs={{0,64},{64,128},{128,192},{192,256},{256,320},{320,384},{384,448},... | collective-permute-start | bytes 4128776 | tf_op jit(solution)/shard_map/ppermute | solution.py:49
  45.9 58.6 %collective-permute-start.3 = (bf16[512,1344]{0,1:T(8,128)(2,1)}, bf16[512,1344]{0,1:T(8,128)(2,1)S(1)}, u32[]{:S(2)}, u32[]{:S(2)}) collective-permute-start(bf16[512,1344]{0,1:T(8,128)(2,1)} %collective-permute-done.1), channel_id=1, source_target_pairs={{0,64},{64,128},{128,192},{192,256},{256,320},{320,384},{384,448},... | collective-permute-start | bytes 4128776 | tf_op jit(solution)/shard_map/ppermute | solution.py:49
  50.3 24.2 %all-to-all-start = ((bf16[4,16,256]{2,0,1:T(4,128)(2,1)}), bf16[4,16,256]{2,0,1:T(4,128)(2,1)S(1)}, u32[]{:S(2)}, u32[]{:S(2)}) async-start(bf16[4,16,256]{2,0,1:T(4,128)(2,1)} %bitcast), calls=%async_computation | async-start | bytes 65536 | tf_op jit(solution)/shard_map/all_to_all | solution.py:80
  58.9 100.3 %all-gather.4.cloned.1.call-start = ((), (), s32[]{:S(2)}) async-start(), calls=%async_computation.1 | async-start | bytes 1310720 | tf_op jit(solution)/shard_map/all_gather | solution.py:75
  101.3 11.8 %collective-permute-start.2 = (bf16[512,1344]{0,1:T(8,128)(2,1)}, bf16[512,1344]{0,1:T(8,128)(2,1)}, u32[]{:S(2)}, u32[]{:S(2)}) collective-permute-start(bf16[512,1344]{0,1:T(8,128)(2,1)} %collective-permute-done.1), channel_id=1, source_target_pairs={{0,32},{32,0},{64,96},{96,64},{128,160},{160,128},{192,224},{224,1... | collective-permute-start | bytes 4128776 | tf_op jit(solution)/shard_map/ppermute | solution.py:55
  103.2 3.2 %copy-start = (bf16[128,4096]{1,0:T(8,128)(2,1)S(1)}, bf16[128,4096]{1,0:T(8,128)(2,1)}, u32[]{:S(2)}) copy-start(bf16[128,4096]{1,0:T(8,128)(2,1)} %all-gather.6.cloned.1.call-done) | copy-start | bytes 3145732
  104.5 21.4 %collective-permute-start.5 = (bf16[512,1344]{0,1:T(8,128)(2,1)S(1)}, bf16[512,1344]{0,1:T(8,128)(2,1)S(1)}, u32[]{:S(2)}, u32[]{:S(2)}) collective-permute-start(bf16[512,1344]{0,1:T(8,128)(2,1)S(1)} %collective-permute-done.3), channel_id=1, source_target_pairs={{0,64},{64,128},{128,192},{192,256},{256,320},{320,384},{384,448},... | collective-permute-start | bytes 4128776 | tf_op jit(solution)/shard_map/ppermute | solution.py:49
  109.7 22.2 %collective-permute-start.4 = (bf16[512,1344]{0,1:T(8,128)(2,1)S(1)}, bf16[512,1344]{0,1:T(8,128)(2,1)S(1)}, u32[]{:S(2)}, u32[]{:S(2)}) collective-permute-start(bf16[512,1344]{0,1:T(8,128)(2,1)S(1)} %collective-permute-done.3), channel_id=1, source_target_pairs={{0,32},{32,0},{64,96},{96,64},{128,160},{160,128},{192,224},{224,1... | collective-permute-start | bytes 4128776 | tf_op jit(solution)/shard_map/ppermute | solution.py:55
  125.9 21.4 %collective-permute-start.7 = (bf16[512,1344]{0,1:T(8,128)(2,1)S(1)}, bf16[512,1344]{0,1:T(8,128)(2,1)S(1)}, u32[]{:S(2)}, u32[]{:S(2)}) collective-permute-start(bf16[512,1344]{0,1:T(8,128)(2,1)S(1)} %collective-permute-done.5), channel_id=1, source_target_pairs={{0,64},{64,128},{128,192},{192,256},{256,320},{320,384},{384,448},... | collective-permute-start | bytes 4128776 | tf_op jit(solution)/shard_map/ppermute | solution.py:49
  129.3 18.7 %collective-permute-start.6 = (bf16[512,1344]{0,1:T(8,128)(2,1)S(1)}, bf16[512,1344]{0,1:T(8,128)(2,1)S(1)}, u32[]{:S(2)}, u32[]{:S(2)}) collective-permute-start(bf16[512,1344]{0,1:T(8,128)(2,1)S(1)} %collective-permute-done.5), channel_id=1, source_target_pairs={{0,32},{32,0},{64,96},{96,64},{128,160},{160,128},{192,224},{224,1... | collective-permute-start | bytes 4128776 | tf_op jit(solution)/shard_map/ppermute | solution.py:55
  148.4 0.9 copy-start.7
  149.3 7.7 %copy-start.3 = (bf16[256,448]{0,1:T(8,128)(2,1)S(1)}, bf16[256,448]{0,1:T(8,128)(2,1)}, u32[]{:S(2)}) copy-start(bf16[256,448]{0,1:T(8,128)(2,1)} %param.10) | copy-start | bytes 688132
  149.3 8.5 %copy-start.4 = (bf16[256,448]{0,1:T(8,128)(2,1)S(1)}, bf16[256,448]{0,1:T(8,128)(2,1)}, u32[]{:S(2)}) copy-start(bf16[256,448]{0,1:T(8,128)(2,1)} %param.12) | copy-start | bytes 688132
  149.5 9.2 %copy-start.5 = (f32[256,448]{0,1:T(8,128)S(1)}, f32[256,448]{0,1:T(8,128)}, u32[]{:S(2)}) copy-start(f32[256,448]{0,1:T(8,128)} %param.13) | copy-start | bytes 1376260
  149.5 9.3 %copy-start.6 = (f32[256,448]{0,1:T(8,128)S(1)}, f32[256,448]{0,1:T(8,128)}, u32[]{:S(2)}) copy-start(f32[256,448]{0,1:T(8,128)} %param.14) | copy-start | bytes 1376260
  149.5 3.6 %collective-permute-start.8 = (bf16[128,896]{0,1:T(8,128)(2,1)S(1)}, bf16[128,896]{0,1:T(8,128)(2,1)}, u32[]{:S(2)}, u32[]{:S(2)}) collective-permute-start(bf16[128,896]{0,1:T(8,128)(2,1)S(1)} %pad_maximum_fusion.2), channel_id=1, source_target_pairs={{0,32},{32,0},{64,96},{96,64},{128,160},{160,128},{192,224},{224,1... | collective-permute-start | bytes 688136 | tf_op jit(solution)/shard_map/ppermute | solution.py:44
  154.9 11.9 %collective-permute-start.9 = (bf16[256,896]{0,1:T(8,128)(2,1)}, bf16[256,896]{0,1:T(8,128)(2,1)}, u32[]{:S(2)}, u32[]{:S(2)}) collective-permute-start(bf16[256,896]{0,1:T(8,128)(2,1)} %pad_maximum_fusion.1), channel_id=1, source_target_pairs={{0,64},{64,128},{128,192},{192,256},{256,320},{320,384},{384,448},... | collective-permute-start | bytes 1376264 | tf_op jit(solution)/shard_map/ppermute | solution.py:49
  166.8 18.2 %collective-permute-start.10 = (bf16[256,896]{0,1:T(8,128)(2,1)}, bf16[256,896]{0,1:T(8,128)(2,1)S(1)}, u32[]{:S(2)}, u32[]{:S(2)}) collective-permute-start(bf16[256,896]{0,1:T(8,128)(2,1)} %collective-permute-done.9), channel_id=1, source_target_pairs={{0,32},{32,0},{64,96},{96,64},{128,160},{160,128},{192,224},{224,1... | collective-permute-start | bytes 1376264 | tf_op jit(solution)/shard_map/ppermute | solution.py:55
  168.7 11.8 %collective-permute-start.11 = (bf16[256,896]{0,1:T(8,128)(2,1)}, bf16[256,896]{0,1:T(8,128)(2,1)S(1)}, u32[]{:S(2)}, u32[]{:S(2)}) collective-permute-start(bf16[256,896]{0,1:T(8,128)(2,1)} %collective-permute-done.9), channel_id=1, source_target_pairs={{0,64},{64,128},{128,192},{192,256},{256,320},{320,384},{384,448},... | collective-permute-start | bytes 1376264 | tf_op jit(solution)/shard_map/ppermute | solution.py:49
  180.5 18.2 %collective-permute-start.12 = (bf16[256,896]{0,1:T(8,128)(2,1)S(1)}, bf16[256,896]{0,1:T(8,128)(2,1)S(1)}, u32[]{:S(2)}, u32[]{:S(2)}) collective-permute-start(bf16[256,896]{0,1:T(8,128)(2,1)S(1)} %collective-permute-done.11), channel_id=1, source_target_pairs={{0,32},{32,0},{64,96},{96,64},{128,160},{160,128},{192,224},{224,1... | collective-permute-start | bytes 1376264 | tf_op jit(solution)/shard_map/ppermute | solution.py:55
  182.5 11.6 %collective-permute-start.13 = (bf16[256,896]{0,1:T(8,128)(2,1)S(1)}, bf16[256,896]{0,1:T(8,128)(2,1)S(1)}, u32[]{:S(2)}, u32[]{:S(2)}) collective-permute-start(bf16[256,896]{0,1:T(8,128)(2,1)S(1)} %collective-permute-done.11), channel_id=1, source_target_pairs={{0,64},{64,128},{128,192},{192,256},{256,320},{320,384},{384,448},... | collective-permute-start | bytes 1376264 | tf_op jit(solution)/shard_map/ppermute | solution.py:49
  194.0 14.1 %collective-permute-start.14 = (bf16[256,896]{0,1:T(8,128)(2,1)S(1)}, bf16[256,896]{0,1:T(8,128)(2,1)S(1)}, u32[]{:S(2)}, u32[]{:S(2)}) collective-permute-start(bf16[256,896]{0,1:T(8,128)(2,1)S(1)} %collective-permute-done.13), channel_id=1, source_target_pairs={{0,32},{32,0},{64,96},{96,64},{128,160},{160,128},{192,224},{224,1... | collective-permute-start | bytes 1376264 | tf_op jit(solution)/shard_map/ppermute | solution.py:55
  196.0 11.6 %collective-permute-start.15 = (bf16[256,896]{0,1:T(8,128)(2,1)S(1)}, bf16[256,896]{0,1:T(8,128)(2,1)S(1)}, u32[]{:S(2)}, u32[]{:S(2)}) collective-permute-start(bf16[256,896]{0,1:T(8,128)(2,1)S(1)} %collective-permute-done.13), channel_id=1, source_target_pairs={{0,64},{64,128},{128,192},{192,256},{256,320},{320,384},{384,448},... | collective-permute-start | bytes 1376264 | tf_op jit(solution)/shard_map/ppermute | solution.py:49
  208.5 1.0 copy-start.1
  208.5 1.0 copy-start.2
Sparse Core Ops, SparseCore 0:
  46.0 30.7 all-gather.5
  101.4 24.4 all-gather.3
where the time goes:
time: 221 us; the launch traced here: 220 us
  waiting for transfers between devices  71.6 us (32%)
  blocking collectives  53.4 us (24%)
  starting transfers between devices  45.2 us (20%)
  matrix products  19 us (9%)
  between operations  15 us (7%)
  local copies, waits for them, and re-layouts  12.3 us (6%)
  other arithmetic  3.25 us (1%)
    ppermute x8, waiting for transfers between devices, chip_ring(): cur = lax.ppermute(cur, DP, ring)  53.8 us
    all_gather x2, blocking collectives, gather_mp(): a = lax.all_gather(a, 'y', axis=0, tiled=True)  53.4 us
    ppermute x8, starting transfers between devices, chip_ring(): cur = lax.ppermute(cur, DP, ring)  20.3 us
    all_to_all x1, waiting for transfers between devices, body(): a2a = lax.all_to_all(t3, DP, split_axis=1, concat_axis=1, tiled=True)  14 us
    ppermute x6, starting transfers between devices, chip_ring(): ex = lax.ppermute(cur, DP, partner)  12.2 us
    dot_general x16, matrix products, body(): term = jnp.dot(part, piece, preferred_element_type=jnp.float32)  10.9 us
    unnamed x28, local copies, waits for them, and re-layouts  8.65 us
    all_to_all x1, starting transfers between devices, body(): a2a = lax.all_to_all(t3, DP, split_axis=1, concat_axis=1, tiled=True)  8.58 us
  transfers between devices with their start and end apart: 19, of which 9 were waited for; matrix products, arithmetic and copies ran while one was open for 12% of the time, Pallas kernels for 0%

commit v1 on v0

--- a/solution.py
+++ b/solution.py
@@ -71,7 +71,8 @@
     d = lax.axis_index(DP)
 
     def gather_mp(a):
-        a = lax.all_gather(a, "y", axis=0, tiled=True)
+        outgoing = jnp.stack([a] * lax.axis_size("y"))
+        a = jnp.concatenate(lax.all_to_all(outgoing, "y", 0, 0), axis=0)
         return lax.all_gather(a, "x", axis=0, tiled=True)
 
     whole = gather_mp(tokens)

time: 221 us -> 204 us (0.923)
  the two profiles are of different devices: /device:TPU:4 before, /device:TPU:2 now
where the time goes in v1:
time: 204 us; the launch traced here: 203 us
  waiting for transfers between devices  71.7 us (35%)
  starting transfers between devices  40.3 us (20%)
  blocking collectives  39.8 us (20%)
  matrix products  19 us (9%)
  between operations  15 us (7%)
  local copies, waits for them, and re-layouts  13.9 us (7%)
  other arithmetic  3.25 us (2%)
    ppermute x8, waiting for transfers between devices, chip_ring(): cur = lax.ppermute(cur, DP, ring)  57.5 us
    all_to_all x1, blocking collectives, body(): a2a = lax.all_to_all(t3, DP, split_axis=1, concat_axis=1, tiled=True)  22.4 us
    ppermute x8, starting transfers between devices, chip_ring(): cur = lax.ppermute(cur, DP, ring)  19.6 us
    all_to_all x1, blocking collectives, gather_mp(): a = jnp.concatenate(lax.all_to_all(outgoing, 'y', 0, 0), axis=0)  17.4 us
    ppermute x6, starting transfers between devices, chip_ring(): ex = lax.ppermute(cur, DP, partner)  11.5 us
    dot_general x16, matrix products, body(): term = jnp.dot(part, piece, preferred_element_type=jnp.float32)  10.9 us
    all_to_all x1, waiting for transfers between devices, gather_mp(): a = jnp.concatenate(lax.all_to_all(outgoing, 'y', 0, 0), axis=0)  10.4 us
    dot_general x16, matrix products, body(): lax.dot_general(part, piece, (((0,), (0,)), ((), ())), preferred_element_...  8.18 us
  transfers between devices with their start and end apart: 19, of which 10 were waited for; matrix products, arithmetic and copies ran while one was open for 14% of the time, Pallas kernels for 0%

profile of v1, /device:TPU:2, one launch (start us, length us, event | category | flops | bytes accessed | tf_op | source)
XLA Modules:
  0.0 203.0 jit_solution(2128038573988500716)
XLA Ops:
  7.2 1.0 constant_dynamic-update-slice_fusion.2
  8.2 1.0 constant_dynamic-update-slice_fusion.1
  9.1 1.0 constant_dynamic-update-slice_fusion
  10.1 1.9 collective-permute-start
  12.0 2.1 %collective-permute-done = bf16[256,1344]{0,1:T(8,128)(2,1)S(1)} collective-permute-done((bf16[256,1344]{0,1:T(8,128)(2,1)S(1)}, bf16[256,1344]{0,1:T(8,128)(2,1)S(1)}, u32[]{:S(2)}, u32[]{:S(2)}) %collective-permute-start) | collective-permute-done | bytes 688160 | tf_op jit(solution)/shard_map/ppermute | solution.py:44
  14.2 4.3 %collective-permute-start.1 = (bf16[512,1344]{0,1:T(8,128)(2,1)S(1)}, bf16[512,1344]{0,1:T(8,128)(2,1)}, u32[]{:S(2)}, u32[]{:S(2)}) collective-permute-start(bf16[512,1344]{0,1:T(8,128)(2,1)S(1)} %pad_maximum_fusion), channel_id=1, source_target_pairs={{0,64},{64,128},{128,192},{192,256},{256,320},{320,384},{384,448},... | collective-permute-start | bytes 4128776 | tf_op jit(solution)/shard_map/ppermute | solution.py:49
  18.6 17.4 %all_to_all.15 = bf16[8,4,4096]{2,1,0:T(4,128)(2,1)S(1)} all-to-all(bf16[8,4,4096]{2,1,0:T(4,128)(2,1)S(1)} %stack.5), channel_id=1, replica_groups=mesh['z'=8,'c'=2,'x'=4,'y'=8] {'y'}, dimensions={0} | all-to-all | bytes 524288 | tf_op jit(solution)/shard_map/all_to_all | solution.py:75
  36.8 4.8 %collective-permute-done.1 = bf16[512,1344]{0,1:T(8,128)(2,1)} collective-permute-done((bf16[512,1344]{0,1:T(8,128)(2,1)S(1)}, bf16[512,1344]{0,1:T(8,128)(2,1)}, u32[]{:S(2)}, u32[]{:S(2)}) %collective-permute-start.1) | collective-permute-done | bytes 1376288 | tf_op jit(solution)/shard_map/ppermute | solution.py:49
  41.6 1.9 collective-permute-start.3
  43.5 22.4 %all_to_all.16 = bf16[4,16,256]{2,0,1:T(4,128)(2,1)S(1)} all-to-all(bf16[4,16,256]{2,0,1:T(4,128)(2,1)S(1)} %bitcast.13), channel_id=1, replica_groups=mesh['z'=8,'c'=2,'x'=4,'y'=8] {'z','c'}, dimensions={1} | all-to-all | bytes 65536 | tf_op jit(solution)/shard_map/all_to_all | solution.py:81
  65.9 0.8 stack.4
  66.7 5.2 %all-to-all-start.1 = ((bf16[8,4,16,256]{3,1,2,0:T(4,128)(2,1)}), bf16[8,4,16,256]{3,1,2,0:T(4,128)(2,1)S(1)}, u32[]{:S(2)}, u32[]{:S(2)}) async-start(bf16[8,4,16,256]{3,1,2,0:T(4,128)(2,1)} %stack.4), calls=%async_computation.1 | async-start | bytes 524288 | tf_op jit(solution)/shard_map/all_to_all | solution.py:75
  73.4 10.4 %all-to-all-done.1 = bf16[8,4,16,256]{3,1,2,0:T(4,128)(2,1)S(1)} async-done(((bf16[8,4,16,256]{3,1,2,0:T(4,128)(2,1)}), bf16[8,4,16,256]{3,1,2,0:T(4,128)(2,1)S(1)}, u32[]{:S(2)}, u32[]{:S(2)}) %all-to-all-start.1) | async-done | bytes 262176 | tf_op jit(solution)/shard_map/all_to_all | solution.py:75
  84.6 1.9 collective-permute-start.2
  86.6 1.3 fusion.108
  87.9 3.4 %collective-permute-start.5 = (bf16[512,1344]{0,1:T(8,128)(2,1)S(1)}, bf16[512,1344]{0,1:T(8,128)(2,1)S(1)}, u32[]{:S(2)}, u32[]{:S(2)}) collective-permute-start(bf16[512,1344]{0,1:T(8,128)(2,1)S(1)} %collective-permute-done.3), channel_id=1, source_target_pairs={{0,64},{64,128},{128,192},{192,256},{256,320},{320,384},{384,448},... | collective-permute-start | bytes 4128776 | tf_op jit(solution)/shard_map/ppermute | solution.py:49
  91.6 1.5 fusion.41
  93.1 1.5 fusion
  94.6 1.9 collective-permute-start.4
  97.2 1.5 fusion.38
  98.7 10.6 %collective-permute-done.5 = bf16[512,1344]{0,1:T(8,128)(2,1)S(1)} collective-permute-done((bf16[512,1344]{0,1:T(8,128)(2,1)S(1)}, bf16[512,1344]{0,1:T(8,128)(2,1)S(1)}, u32[]{:S(2)}, u32[]{:S(2)}) %collective-permute-start.5) | collective-permute-done | bytes 1376288 | tf_op jit(solution)/shard_map/ppermute | solution.py:49
  109.3 2.2 %collective-permute-start.7 = (bf16[512,1344]{0,1:T(8,128)(2,1)S(1)}, bf16[512,1344]{0,1:T(8,128)(2,1)S(1)}, u32[]{:S(2)}, u32[]{:S(2)}) collective-permute-start(bf16[512,1344]{0,1:T(8,128)(2,1)S(1)} %collective-permute-done.5), channel_id=1, source_target_pairs={{0,64},{64,128},{128,192},{192,256},{256,320},{320,384},{384,448},... | collective-permute-start | bytes 4128776 | tf_op jit(solution)/shard_map/ppermute | solution.py:49
  111.5 1.5 fusion.3
  112.9 1.9 collective-permute-start.6
  116.3 14.4 %collective-permute-done.7 = bf16[512,1344]{0,1:T(8,128)(2,1)S(1)} collective-permute-done((bf16[512,1344]{0,1:T(8,128)(2,1)S(1)}, bf16[512,1344]{0,1:T(8,128)(2,1)S(1)}, u32[]{:S(2)}, u32[]{:S(2)}) %collective-permute-start.7) | collective-permute-done | bytes 1376288 | tf_op jit(solution)/shard_map/ppermute | solution.py:49
  132.9 2.1 %collective-permute-start.8 = (bf16[128,896]{0,1:T(8,128)(2,1)S(1)}, bf16[128,896]{0,1:T(8,128)(2,1)}, u32[]{:S(2)}, u32[]{:S(2)}) collective-permute-start(bf16[128,896]{0,1:T(8,128)(2,1)S(1)} %pad_maximum_fusion.2), channel_id=1, source_target_pairs={{0,32},{32,0},{64,96},{96,64},{128,160},{160,128},{192,224},{224,1... | collective-permute-start | bytes 688136 | tf_op jit(solution)/shard_map/ppermute | solution.py:44
  134.9 1.6 collective-permute-done.8
  136.5 1.8 pad_maximum_fusion.1
  138.3 1.9 collective-permute-start.9
  140.3 0.8 copy.42
  141.2 0.8 copy.47
  142.5 1.8 copy.52
  144.9 1.3 convolution_add_fusion.9
  146.2 4.0 %collective-permute-done.9 = bf16[256,896]{0,1:T(8,128)(2,1)} collective-permute-done((bf16[256,896]{0,1:T(8,128)(2,1)}, bf16[256,896]{0,1:T(8,128)(2,1)}, u32[]{:S(2)}, u32[]{:S(2)}) %collective-permute-start.9) | collective-permute-done | bytes 458784 | tf_op jit(solution)/shard_map/ppermute | solution.py:49
  150.2 1.9 collective-permute-start.10
  152.1 1.9 collective-permute-start.11
  154.0 1.3 fusion.75
  155.3 1.3 fusion.19
  156.5 7.3 %collective-permute-done.11 = bf16[256,896]{0,1:T(8,128)(2,1)S(1)} collective-permute-done((bf16[256,896]{0,1:T(8,128)(2,1)}, bf16[256,896]{0,1:T(8,128)(2,1)S(1)}, u32[]{:S(2)}, u32[]{:S(2)}) %collective-permute-start.11) | collective-permute-done | bytes 458784 | tf_op jit(solution)/shard_map/ppermute | solution.py:49
  163.9 1.9 collective-permute-start.12
  165.8 1.9 collective-permute-start.13
  169.1 8.3 %collective-permute-done.13 = bf16[256,896]{0,1:T(8,128)(2,1)S(1)} collective-permute-done((bf16[256,896]{0,1:T(8,128)(2,1)S(1)}, bf16[256,896]{0,1:T(8,128)(2,1)S(1)}, u32[]{:S(2)}, u32[]{:S(2)}) %collective-permute-start.13) | collective-permute-done | bytes 458784 | tf_op jit(solution)/shard_map/ppermute | solution.py:49
  177.4 1.9 collective-permute-start.14
  179.3 2.1 %collective-permute-start.15 = (bf16[256,896]{0,1:T(8,128)(2,1)S(1)}, bf16[256,896]{0,1:T(8,128)(2,1)S(1)}, u32[]{:S(2)}, u32[]{:S(2)}) collective-permute-start(bf16[256,896]{0,1:T(8,128)(2,1)S(1)} %collective-permute-done.13), channel_id=1, source_target_pairs={{0,64},{64,128},{128,192},{192,256},{256,320},{320,384},{384,448},... | collective-permute-start | bytes 1376264 | tf_op jit(solution)/shard_map/ppermute | solution.py:49
  182.8 8.1 %collective-permute-done.15 = bf16[256,896]{0,1:T(8,128)(2,1)S(1)} collective-permute-done((bf16[256,896]{0,1:T(8,128)(2,1)S(1)}, bf16[256,896]{0,1:T(8,128)(2,1)S(1)}, u32[]{:S(2)}, u32[]{:S(2)}) %collective-permute-start.15) | collective-permute-done | bytes 458784 | tf_op jit(solution)/shard_map/ppermute | solution.py:49
  193.5 1.0 copy.49
  194.4 1.0 copy.50
  195.4 0.8 copy.48
  (69 shorter events, 13.9 us)
Async XLA Ops:
  7.2 79.4 %all-gather.5.cloned.1.call-start = ((), (), s32[]{:S(2)}) async-start(), calls=%async_computation.4 | async-start | bytes 1310720 | tf_op jit(solution)/shard_map/all_gather | solution.py:76
  10.1 8.5 %copy-start.7 = (bf16[4,4096]{1,0:T(4,128)(2,1)S(1)}, bf16[4,4096]{1,0:T(4,128)(2,1)}, u32[]{:S(2)}) copy-start(bf16[4,4096]{1,0:T(4,128)(2,1)} %param.8) | copy-start | bytes 98308
  10.1 4.0 %collective-permute-start = (bf16[256,1344]{0,1:T(8,128)(2,1)S(1)}, bf16[256,1344]{0,1:T(8,128)(2,1)S(1)}, u32[]{:S(2)}, u32[]{:S(2)}) collective-permute-start(bf16[256,1344]{0,1:T(8,128)(2,1)S(1)} %constant_dynamic-update-slice_fusion), channel_id=1, source_target_pairs={{0,32},{32,0},{64,96},{96,64},{128,160},{160,128},{192,224},{224,1... | collective-permute-start | bytes 2064392 | tf_op jit(solution)/shard_map/ppermute | solution.py:44
  14.2 27.3 %collective-permute-start.1 = (bf16[512,1344]{0,1:T(8,128)(2,1)S(1)}, bf16[512,1344]{0,1:T(8,128)(2,1)}, u32[]{:S(2)}, u32[]{:S(2)}) collective-permute-start(bf16[512,1344]{0,1:T(8,128)(2,1)S(1)} %pad_maximum_fusion), channel_id=1, source_target_pairs={{0,64},{64,128},{128,192},{192,256},{256,320},{320,384},{384,448},... | collective-permute-start | bytes 4128776 | tf_op jit(solution)/shard_map/ppermute | solution.py:49
  18.6 53.6 %copy-start.9 = (s32[16]{0:T(128)S(1)}, s32[16]{0:T(128)}, u32[]{:S(2)}) copy-start(s32[16]{0:T(128)} %param.15) | copy-start | bytes 196
  41.6 46.3 %collective-permute-start.3 = (bf16[512,1344]{0,1:T(8,128)(2,1)}, bf16[512,1344]{0,1:T(8,128)(2,1)S(1)}, u32[]{:S(2)}, u32[]{:S(2)}) collective-permute-start(bf16[512,1344]{0,1:T(8,128)(2,1)} %collective-permute-done.1), channel_id=1, source_target_pairs={{0,64},{64,128},{128,192},{192,256},{256,320},{320,384},{384,448},... | collective-permute-start | bytes 4128776 | tf_op jit(solution)/shard_map/ppermute | solution.py:49
  66.7 17.2 %all-to-all-start.1 = ((bf16[8,4,16,256]{3,1,2,0:T(4,128)(2,1)}), bf16[8,4,16,256]{3,1,2,0:T(4,128)(2,1)S(1)}, u32[]{:S(2)}, u32[]{:S(2)}) async-start(bf16[8,4,16,256]{3,1,2,0:T(4,128)(2,1)} %stack.4), calls=%async_computation.1 | async-start | bytes 524288 | tf_op jit(solution)/shard_map/all_to_all | solution.py:75
  71.9 70.7 %all-gather.3.cloned.1.call-start = ((), (), s32[]{:S(2)}) async-start(), calls=%async_computation.3 | async-start | bytes 1310720 | tf_op jit(solution)/shard_map/all_gather | solution.py:76
  84.6 12.6 %collective-permute-start.2 = (bf16[512,1344]{0,1:T(8,128)(2,1)}, bf16[512,1344]{0,1:T(8,128)(2,1)}, u32[]{:S(2)}, u32[]{:S(2)}) collective-permute-start(bf16[512,1344]{0,1:T(8,128)(2,1)} %collective-permute-done.1), channel_id=1, source_target_pairs={{0,32},{32,0},{64,96},{96,64},{128,160},{160,128},{192,224},{224,1... | collective-permute-start | bytes 4128776 | tf_op jit(solution)/shard_map/ppermute | solution.py:55
  86.6 4.7 %copy-start = (bf16[128,4096]{1,0:T(8,128)(2,1)S(1)}, bf16[128,4096]{1,0:T(8,128)(2,1)}, u32[]{:S(2)}) copy-start(bf16[128,4096]{1,0:T(8,128)(2,1)} %all-gather.5.cloned.1.call-done) | copy-start | bytes 3145732
  87.9 21.4 %collective-permute-start.5 = (bf16[512,1344]{0,1:T(8,128)(2,1)S(1)}, bf16[512,1344]{0,1:T(8,128)(2,1)S(1)}, u32[]{:S(2)}, u32[]{:S(2)}) collective-permute-start(bf16[512,1344]{0,1:T(8,128)(2,1)S(1)} %collective-permute-done.3), channel_id=1, source_target_pairs={{0,64},{64,128},{128,192},{192,256},{256,320},{320,384},{384,448},... | collective-permute-start | bytes 4128776 | tf_op jit(solution)/shard_map/ppermute | solution.py:49
  94.6 21.0 %collective-permute-start.4 = (bf16[512,1344]{0,1:T(8,128)(2,1)S(1)}, bf16[512,1344]{0,1:T(8,128)(2,1)S(1)}, u32[]{:S(2)}, u32[]{:S(2)}) collective-permute-start(bf16[512,1344]{0,1:T(8,128)(2,1)S(1)} %collective-permute-done.3), channel_id=1, source_target_pairs={{0,32},{32,0},{64,96},{96,64},{128,160},{160,128},{192,224},{224,1... | collective-permute-start | bytes 4128776 | tf_op jit(solution)/shard_map/ppermute | solution.py:55
  109.3 21.4 %collective-permute-start.7 = (bf16[512,1344]{0,1:T(8,128)(2,1)S(1)}, bf16[512,1344]{0,1:T(8,128)(2,1)S(1)}, u32[]{:S(2)}, u32[]{:S(2)}) collective-permute-start(bf16[512,1344]{0,1:T(8,128)(2,1)S(1)} %collective-permute-done.5), channel_id=1, source_target_pairs={{0,64},{64,128},{128,192},{192,256},{256,320},{320,384},{384,448},... | collective-permute-start | bytes 4128776 | tf_op jit(solution)/shard_map/ppermute | solution.py:49
  112.9 18.5 %collective-permute-start.6 = (bf16[512,1344]{0,1:T(8,128)(2,1)S(1)}, bf16[512,1344]{0,1:T(8,128)(2,1)S(1)}, u32[]{:S(2)}, u32[]{:S(2)}) collective-permute-start(bf16[512,1344]{0,1:T(8,128)(2,1)S(1)} %collective-permute-done.5), channel_id=1, source_target_pairs={{0,32},{32,0},{64,96},{96,64},{128,160},{160,128},{192,224},{224,1... | collective-permute-start | bytes 4128776 | tf_op jit(solution)/shard_map/ppermute | solution.py:55
  131.7 0.9 copy-start.8
  132.6 7.7 %copy-start.3 = (bf16[256,448]{0,1:T(8,128)(2,1)S(1)}, bf16[256,448]{0,1:T(8,128)(2,1)}, u32[]{:S(2)}) copy-start(bf16[256,448]{0,1:T(8,128)(2,1)} %param.10) | copy-start | bytes 688132
  132.6 8.5 %copy-start.4 = (bf16[256,448]{0,1:T(8,128)(2,1)S(1)}, bf16[256,448]{0,1:T(8,128)(2,1)}, u32[]{:S(2)}) copy-start(bf16[256,448]{0,1:T(8,128)(2,1)} %param.12) | copy-start | bytes 688132
  132.8 9.2 %copy-start.5 = (f32[256,448]{0,1:T(8,128)S(1)}, f32[256,448]{0,1:T(8,128)}, u32[]{:S(2)}) copy-start(f32[256,448]{0,1:T(8,128)} %param.13) | copy-start | bytes 1376260
  132.9 9.3 %copy-start.6 = (f32[256,448]{0,1:T(8,128)S(1)}, f32[256,448]{0,1:T(8,128)}, u32[]{:S(2)}) copy-start(f32[256,448]{0,1:T(8,128)} %param.14) | copy-start | bytes 1376260
  132.9 3.6 %collective-permute-start.8 = (bf16[128,896]{0,1:T(8,128)(2,1)S(1)}, bf16[128,896]{0,1:T(8,128)(2,1)}, u32[]{:S(2)}, u32[]{:S(2)}) collective-permute-start(bf16[128,896]{0,1:T(8,128)(2,1)S(1)} %pad_maximum_fusion.2), channel_id=1, source_target_pairs={{0,32},{32,0},{64,96},{96,64},{128,160},{160,128},{192,224},{224,1... | collective-permute-start | bytes 688136 | tf_op jit(solution)/shard_map/ppermute | solution.py:44
  138.3 11.9 %collective-permute-start.9 = (bf16[256,896]{0,1:T(8,128)(2,1)}, bf16[256,896]{0,1:T(8,128)(2,1)}, u32[]{:S(2)}, u32[]{:S(2)}) collective-permute-start(bf16[256,896]{0,1:T(8,128)(2,1)} %pad_maximum_fusion.1), channel_id=1, source_target_pairs={{0,64},{64,128},{128,192},{192,256},{256,320},{320,384},{384,448},... | collective-permute-start | bytes 1376264 | tf_op jit(solution)/shard_map/ppermute | solution.py:49
  150.2 18.2 %collective-permute-start.10 = (bf16[256,896]{0,1:T(8,128)(2,1)}, bf16[256,896]{0,1:T(8,128)(2,1)S(1)}, u32[]{:S(2)}, u32[]{:S(2)}) collective-permute-start(bf16[256,896]{0,1:T(8,128)(2,1)} %collective-permute-done.9), channel_id=1, source_target_pairs={{0,32},{32,0},{64,96},{96,64},{128,160},{160,128},{192,224},{224,1... | collective-permute-start | bytes 1376264 | tf_op jit(solution)/shard_map/ppermute | solution.py:55
  152.1 11.8 %collective-permute-start.11 = (bf16[256,896]{0,1:T(8,128)(2,1)}, bf16[256,896]{0,1:T(8,128)(2,1)S(1)}, u32[]{:S(2)}, u32[]{:S(2)}) collective-permute-start(bf16[256,896]{0,1:T(8,128)(2,1)} %collective-permute-done.9), channel_id=1, source_target_pairs={{0,64},{64,128},{128,192},{192,256},{256,320},{320,384},{384,448},... | collective-permute-start | bytes 1376264 | tf_op jit(solution)/shard_map/ppermute | solution.py:49
  163.9 18.2 %collective-permute-start.12 = (bf16[256,896]{0,1:T(8,128)(2,1)S(1)}, bf16[256,896]{0,1:T(8,128)(2,1)S(1)}, u32[]{:S(2)}, u32[]{:S(2)}) collective-permute-start(bf16[256,896]{0,1:T(8,128)(2,1)S(1)} %collective-permute-done.11), channel_id=1, source_target_pairs={{0,32},{32,0},{64,96},{96,64},{128,160},{160,128},{192,224},{224,1... | collective-permute-start | bytes 1376264 | tf_op jit(solution)/shard_map/ppermute | solution.py:55
  165.8 11.6 %collective-permute-start.13 = (bf16[256,896]{0,1:T(8,128)(2,1)S(1)}, bf16[256,896]{0,1:T(8,128)(2,1)S(1)}, u32[]{:S(2)}, u32[]{:S(2)}) collective-permute-start(bf16[256,896]{0,1:T(8,128)(2,1)S(1)} %collective-permute-done.11), channel_id=1, source_target_pairs={{0,64},{64,128},{128,192},{192,256},{256,320},{320,384},{384,448},... | collective-permute-start | bytes 1376264 | tf_op jit(solution)/shard_map/ppermute | solution.py:49
  177.4 14.1 %collective-permute-start.14 = (bf16[256,896]{0,1:T(8,128)(2,1)S(1)}, bf16[256,896]{0,1:T(8,128)(2,1)S(1)}, u32[]{:S(2)}, u32[]{:S(2)}) collective-permute-start(bf16[256,896]{0,1:T(8,128)(2,1)S(1)} %collective-permute-done.13), channel_id=1, source_target_pairs={{0,32},{32,0},{64,96},{96,64},{128,160},{160,128},{192,224},{224,1... | collective-permute-start | bytes 1376264 | tf_op jit(solution)/shard_map/ppermute | solution.py:55
  179.3 11.6 %collective-permute-start.15 = (bf16[256,896]{0,1:T(8,128)(2,1)S(1)}, bf16[256,896]{0,1:T(8,128)(2,1)S(1)}, u32[]{:S(2)}, u32[]{:S(2)}) collective-permute-start(bf16[256,896]{0,1:T(8,128)(2,1)S(1)} %collective-permute-done.13), channel_id=1, source_target_pairs={{0,64},{64,128},{128,192},{192,256},{256,320},{320,384},{384,448},... | collective-permute-start | bytes 1376264 | tf_op jit(solution)/shard_map/ppermute | solution.py:49
  191.9 1.0 copy-start.1
  191.9 1.0 copy-start.2
Sparse Core Ops, SparseCore 0:
  37.0 26.8 all-gather.4
  84.7 21.4 all-gather.2
